TPU v7x, 32 devices: a whole 2x2x4 slice. The times are simulated.
32 devices in a mesh: groups: 2 (over y), cent: 4 (over z), dp: 2 (over x), sub: 2 (over core).
Axes of the slice: x: 2, y: 2, z: 4, core: 2. Of those that a mesh axis runs over, the one named last changes fastest.
Arguments:
- embeddings: bfloat16 [1024, 768], P(('groups', 'cent', 'dp', 'sub')), parts along dimension 0, may hold values from -6 to 6
- weights: int32 [1024], P(('groups', 'cent', 'dp', 'sub')), parts along dimension 0, may hold values from 1 to 4
- centroids: bfloat16 [16384, 768], P(('groups', 'cent')), parts along dimension 0, may hold values from -6 to 6
- inverse_temp: float32 [1], replicated, may hold values from 16 to 256
Outputs:
- centroid_sums: float32 [16384, 768], P(('groups', 'cent', 'dp', 'sub')), parts along dimension 0
- renormed: bfloat16 [16384, 768], P(('groups', 'cent', 'dp', 'sub')), parts along dimension 0
- objective: float32 [1024], P(('groups', 'cent', 'dp', 'sub')), parts along dimension 0
There are 2 independent parts, one for each index of `groups`. A program takes and returns all parts, laid end to end along the dimension named above; an argument that names none is the same for every part. Nothing has to cross between parts.
All inputs are finite; a program needn't handle non-finite values.
Results may differ from a plain program's by a relative error of at most 0.0075.
The roundings to bfloat16 on the way count: a program that leaves them out, or rounds other values in their place, can miss the bound.
Values may be sent and summed in bfloat16 or wider, within the bound.
No kernel may reach another device: no remote copies, remote signals or barrier semaphores. Data moves between devices by JAX's collectives and lax.ppermute only.
A program may use at most 64 MiB of HBM per device.

v0:
```python
import jax
import jax.numpy as jnp
from jax import lax
from jax.sharding import PartitionSpec as P


def normalize(values):
    floats = values.astype(jnp.float32)
    return floats * lax.rsqrt(jnp.sum(floats * floats, axis=-1, keepdims=True) + 1e-06)


def shards(embeddings, weights, centroids, inverse_temp):
    sharpness = inverse_temp[0]
    unit_rows = normalize(embeddings).astype(jnp.bfloat16)
    unit_panel = normalize(centroids).astype(jnp.bfloat16)
    gathered_rows, gathered_weights = (
        lax.all_gather(unit_rows, "cent", axis=0, tiled=True),
        lax.all_gather(weights, "cent", axis=0, tiled=True),
    )
    scores = (
        lax.dot_general(
            gathered_rows, unit_panel, (((1,), (1,)), ((), ())), preferred_element_type=jnp.float32
        )
        * sharpness
    )
    local_peak = jnp.max(scores, axis=1)
    row_peak = lax.pmax(local_peak, "cent")
    row_total = lax.psum(jnp.sum(jnp.exp(scores - row_peak[:, None]), axis=1), "cent")
    log_sum = row_peak + jnp.log(row_total)
    weight_float = gathered_weights.astype(jnp.float32)
    responsibility = (weight_float[:, None] * jnp.exp(scores - log_sum[:, None])).astype(
        jnp.bfloat16
    )
    partial_value = lax.dot_general(
        responsibility, gathered_rows, (((0,), (0,)), ((), ())), preferred_element_type=jnp.float32
    ).astype(jnp.bfloat16)
    ones_row = jnp.ones((1, responsibility.shape[0]), jnp.bfloat16)
    weight_mass = jnp.dot(ones_row, responsibility, preferred_element_type=jnp.float32)[0].astype(
        jnp.bfloat16
    )
    own_count = centroids.shape[0] // lax.axis_size(("dp", "sub"))
    offset = lax.axis_index(("dp", "sub")) * own_count
    panel_sums, panel_mass = (
        lax.psum(partial_value, ("dp", "sub")).astype(jnp.float32),
        lax.psum(weight_mass, ("dp", "sub")).astype(jnp.float32),
    )
    centroid_sums = lax.dynamic_slice_in_dim(panel_sums, offset, own_count, 0)
    own_mass = lax.dynamic_slice_in_dim(panel_mass, offset, own_count, 0)
    own_cents = lax.dynamic_slice_in_dim(unit_panel, offset, own_count, 0).astype(jnp.float32)
    moved = own_cents + centroid_sums / (own_mass + 1.0)[:, None]
    renormed = normalize(moved).astype(jnp.bfloat16)
    row_offset = lax.axis_index("cent") * embeddings.shape[0]
    weighted_log_sum = weight_float * log_sum / sharpness
    objective = lax.dynamic_slice_in_dim(weighted_log_sum, row_offset, embeddings.shape[0], 0)
    return (centroid_sums, renormed, objective)


def solution(mesh):
    in_specs = (
        P(("groups", "cent", "dp", "sub"), None),
        P(("groups", "cent", "dp", "sub")),
        P(("groups", "cent"), None),
        P(),
    )
    out_specs = (
        P(("groups", "cent", "dp", "sub"), None),
        P(("groups", "cent", "dp", "sub"), None),
        P(("groups", "cent", "dp", "sub")),
    )
    return jax.shard_map(shards, mesh=mesh, in_specs=in_specs, out_specs=out_specs, check_vma=False)
```

profile of v0, /device:TPU:0, one launch (start us, length us, event | category | flops | bytes accessed | tf_op | source)
XLA Modules:
  0.0 144.0 jit_solution(1710212666322466163)
XLA Ops:
  7.2 0.0 copy-start.3
  7.2 0.0 all-reduce.3.cloned.1.call-start
  7.9 0.9 fusion.2
  8.8 1.2 dynamic-slice
  10.7 0.9 dynamic-update-slice
  11.6 9.9 %all-reduce = s32[128]{0:T(128)S(1)} all-reduce(s32[128]{0:T(128)S(1)} %dynamic-update-slice), channel_id=1, replica_groups=mesh['groups'=2,'cent'=4,'dp'=2,'sub'=2] {'cent'}, use_global_device_ids=true, to_apply=%add | all-reduce | flops 128 | bytes 1024
  21.5 0.0 copy-start
  21.5 2.7 %fusion = f32[2048]{0:T(1024)S(1)} fusion(bf16[2048,768]{1,0:T(8,128)(2,1)} %param.6), kind=kLoop, calls=%fused_computation.2 | loop fusion | flops 4716544 | bytes 3153920 | tf_op jit(solution)/shard_map/reduce_sum | solution.py:9
  24.2 0.0 copy-done.3
  24.2 0.1 fusion.3
  24.3 13.6 %all_gather.7 = bf16[128,768]{1,0:T(8,128)(2,1)S(1)} all-gather(bf16[32,768]{1,0:T(8,128)(2,1)S(1)} %fusion.3), channel_id=1, replica_groups=mesh['groups'=2,'cent'=4,'dp'=2,'sub'=2] {'cent'}, dimensions={0}, use_global_device_ids=true | all-gather | bytes 245760 | tf_op jit(solution)/shard_map/all_gather | solution.py:17
  37.9 0.0 copy-done
  37.9 0.6 fusion.1
  38.4 2.1 %fusion.7 = (f32[128]{0:T(128)S(1)}, f32[128,2048]{1,0:T(8,128)}) fusion(f32[]{:T(128)} %bitcast.8, bf16[128,768]{1,0:T(8,128)(2,1)S(1)} %all_gather.7, bf16[2048,768]{1,0:T(8,128)(2,1)S(1)} %fusion.1), kind=kOutput, calls=%fused_computation.25 | convolution fusion | flops 403177344 | bytes 4391428 | tf_op jit(solution)/shard_map/dot_general | solution.py:21
  40.6 10.4 %pmax.7 = f32[128]{0:T(128)S(1)} all-reduce(f32[128]{0:T(128)S(1)} %get-tuple-element.7), channel_id=1, replica_groups=mesh['groups'=2,'cent'=4,'dp'=2,'sub'=2] {'cent'}, use_global_device_ids=true, to_apply=%region_3.0 | all-reduce | flops 128 | bytes 1024 | tf_op jit(solution)/shard_map/pmax | solution.py:27
  51.0 1.5 %exponential_reduce_fusion = f32[128]{0:T(128)S(1)} fusion(f32[128,2048]{1,0:T(8,128)} %get-tuple-element.8, f32[128]{0:T(128)S(1)} %pmax.7), kind=kLoop, calls=%fused_computation.10 | loop fusion | flops 524160 | bytes 1049600 | tf_op jit(solution)/shard_map/reduce_sum | solution.py:28
  52.5 8.4 %psum.21 = f32[128]{0:T(128)S(1)} all-reduce(f32[128]{0:T(128)S(1)} %exponential_reduce_fusion), channel_id=1, replica_groups=mesh['groups'=2,'cent'=4,'dp'=2,'sub'=2] {'cent'}, use_global_device_ids=true, to_apply=%region_5.0 | all-reduce | flops 128 | bytes 1024 | tf_op jit(solution)/shard_map/psum | solution.py:28
  60.9 1.5 %multiply_convert_fusion.1 = bf16[128,2048]{1,0:T(8,128)(2,1)S(1)} fusion(f32[128,2048]{1,0:T(8,128)} %get-tuple-element.8, f32[128]{0:T(128)S(1)} %get-tuple-element.4, f32[128]{0:T(128)S(1)} %convert_element_type.36), kind=kLoop, calls=%fused_computation.9 | loop fusion | flops 786432 | bytes 1573888 | tf_op jit(solution)/shard_map/convert_element_type | solution.py:31
  62.4 0.0 copy-start.2
  62.4 0.8 copy-done.2
  63.2 2.7 %convolution_convert_fusion = bf16[2048,768]{1,0:T(8,128)(2,1)} fusion(bf16[128,2048]{1,0:T(8,128)(2,1)S(1)} %multiply_convert_fusion.1, bf16[128,768]{1,0:T(8,128)(2,1)S(1)} %all_gather.7), kind=kOutput, calls=%fused_computation.4 | convolution fusion | flops 404226048 | bytes 3866624 | tf_op jit(solution)/shard_map/dot_general | solution.py:34
  65.9 0.0 all-reduce.3.cloned.1.call-update
  65.9 1.2 fusion.4
  67.2 0.6 dynamic_slice.15
  67.7 5.6 %psum.23 = bf16[2048]{0:T(1024)(128)(2,1)S(1)} all-reduce(bf16[2048]{0:T(1024)(128)(2,1)S(1)} %convert_element_type.45), channel_id=1, replica_groups=mesh['groups'=2,'cent'=4,'dp'=2,'sub'=2] {'dp','sub'}, use_global_device_ids=true, to_apply=%region_7.0 | all-reduce | flops 2048 | bytes 8192 | tf_op jit(solution)/shard_map/psum | solution.py:45
  73.4 0.1 convert_add_fusion
  73.5 60.7 %all-reduce.3.cloned.1.call-done = bf16[2048,768]{1,0:T(8,128)(2,1)} async-done(((bf16[2048,768]{1,0:T(8,128)(2,1)}), bf16[2048,768]{1,0:T(8,128)(2,1)}) %all-reduce.3.cloned.1.call-update) | async-done | bytes 3145744 | tf_op jit(solution)/shard_map/psum | solution.py:44
  134.2 1.6 %multiply_reduce_fusion = (f32[512]{0:T(512)S(1)}, f32[512,768]{1,0:T(8,128)S(1)}) fusion(f32[512]{0:T(512)S(1)} %convert_add_fusion, bf16[2048,768]{1,0:T(8,128)(2,1)S(1)} %fusion.1, s32[]{:T(128)S(6)} %select_n.8, bf16[2048,768]{1,0:T(8,128)(2,1)} %all-reduce.3.cloned.1.call-done), kind=kLoop, calls=%fused_computation.7 | loop fusion | flops 2358784 | bytes 3149828 | tf_op jit(solution)/shard_map/reduce_sum | solution.py:9
  135.8 0.0 copy-start.1
  135.8 1.4 multiply_convert_fusion
  137.2 0.0 copy-done.1
  (7 shorter events, 0.0 us)
Async XLA Ops:
  7.2 17.0 %copy-start.3 = (bf16[32,768]{1,0:T(8,128)(2,1)S(1)}, bf16[32,768]{1,0:T(8,128)(2,1)}, u32[]{:S(2)}) copy-start(bf16[32,768]{1,0:T(8,128)(2,1)} %param.4) | copy-start | bytes 147460
  7.2 127.0 %all-reduce.3.cloned.1.call-start = ((), (), s32[]{:S(2)}) async-start(), calls=%async_computation | async-start | bytes 6291456 | tf_op jit(solution)/shard_map/psum | solution.py:44
  21.5 16.4 %copy-start = (bf16[2048,768]{1,0:T(8,128)(2,1)S(1)}, bf16[2048,768]{1,0:T(8,128)(2,1)}, u32[]{:S(2)}) copy-start(bf16[2048,768]{1,0:T(8,128)(2,1)} %param.6) | copy-start | bytes 9437188
  62.4 0.8 copy-start.2
  135.8 1.4 copy-start.1
Sparse Core Ops, SparseCore 0:
  66.0 68.1 all-reduce.2
where the time goes:
time: 145 us; the launch traced here: 144 us
  waiting for transfers between devices  60.8 us (42%)
  blocking collectives  47.9 us (33%)
  between operations  15.4 us (11%)
  other arithmetic  10.4 us (7%)
  matrix products  6.06 us (4%)
  local copies, waits for them, and re-layouts  3.49 us (2%)
    psum x1, waiting for transfers between devices, shards(): lax.psum(partial_value, ('dp', 'sub')).astype(jnp.float32)  60.7 us
    all_gather x1, blocking collectives, shards(): lax.all_gather(unit_rows, 'cent', axis=0, tiled=True)  13.6 us
    pmax x1, blocking collectives, shards(): row_peak = lax.pmax(local_peak, 'cent')  10.4 us
    unnamed x1, blocking collectives  9.89 us
    psum x1, blocking collectives, shards(): lax.psum(jnp.sum(jnp.exp(scores - row_peak[:, None]), axis=1), 'cent')  8.37 us
    psum x1, blocking collectives, shards(): lax.psum(weight_mass, ('dp', 'sub')).astype(jnp.float32)  5.64 us
    reduce_sum x3, other arithmetic, normalize(): jnp.sum(floats * floats, axis=-1, keepdims=True) + 1e-06  5.22 us
    unnamed x11, local copies, waits for them, and re-layouts  2.9 us
  transfers between devices with their start and end apart: 1, of which 1 were waited for; matrix products, arithmetic and copies ran while one was open for 1% of the time, Pallas kernels for 0%

commit v1 on v0

--- a/solution.py
+++ b/solution.py
@@ -2,6 +2,12 @@
 import jax.numpy as jnp
 from jax import lax
 from jax.sharding import PartitionSpec as P
+
+
+def write_the_clusters(xx, k_dim):
+    fresh = list(xx.shape[1:])
+    fresh[k_dim] *= xx.shape[0]
+    return jnp.moveaxis(xx, 0, k_dim).reshape(fresh)
 
 
 def normalize(values):
@@ -10,11 +16,33 @@
 
 
 def shards(embeddings, weights, centroids, inverse_temp):
+
+    def save_rates(comm_axis, array_dim, m):
+        wide_n = jax.lax.axis_size(comm_axis)
+        made = [(src_i, (src_i + 1) % wide_n) for src_i in range(wide_n)]
+        pool = [(idx, p) for p, idx in made]
+        row_out, carry_out = ([], [])
+        for dev_j in range(wide_n - 1):
+            if dev_j % 2 == 0:
+                p_next = jax.lax.ppermute(
+                    row_out[-1] if row_out else m, axis_name=comm_axis, perm=made
+                )
+                row_out.append(p_next)
+            else:
+                carry_out.append(
+                    jax.lax.ppermute(carry_out[-1] if carry_out else m, comm_axis, perm=pool)
+                )
+        x_next = jnp.stack([*row_out[::-1], m, *carry_out])
+        known = jax.lax.axis_index(comm_axis)
+        t1 = known - len(row_out)
+        x_next = x_next[(jnp.arange(wide_n) - t1) % wide_n]
+        return write_the_clusters(x_next, array_dim)
+
     sharpness = inverse_temp[0]
     unit_rows = normalize(embeddings).astype(jnp.bfloat16)
     unit_panel = normalize(centroids).astype(jnp.bfloat16)
     gathered_rows, gathered_weights = (
-        lax.all_gather(unit_rows, "cent", axis=0, tiled=True),
+        save_rates("cent", 0, unit_rows),
         lax.all_gather(weights, "cent", axis=0, tiled=True),
     )
     scores = (

time: 145 us -> 137 us (0.945)
  blocking collectives: 47.9 us -> 33.1 us
  starting transfers between devices: 0.04 us -> 5.1 us
  other arithmetic: 10.4 us -> 12.1 us
    all_gather x1 -> x0, blocking collectives: 13.6 us -> none  [shards(): lax.all_gather(unit_rows, 'cent', axis=0, tiled=True)]
    ppermute x0 -> x3, starting transfers between devices: none -> 5.06 us  [the longest x1 5.05 us: save_rates(): jax.lax.ppermute(carry_out[-1] if carry_out else m, comm_axis, perm=pool)]
    ppermute x0 -> x3, waiting for transfers between devices: none -> 1.58 us  [the longest x2 1.57 us: save_rates(): jax.lax.ppermute(row_out[-1] if row_out else m, axis_name=comm_axis, perm...]
    unnamed x11 -> x13, local copies, waits for them, and re-layouts: 2.9 us -> 1.72 us
  transfers between devices with their start and end apart: 1 -> 4, of which waited for: 1 -> 2; matrix products, arithmetic and copies ran while one was open for 1% -> 5% of each run, Pallas kernels for 0% -> 0%
where the time goes in v1:
time: 137 us
  waiting for transfers between devices  61.9 us (45%)
  blocking collectives  33.1 us (24%)
  between operations  15.5 us (11%)
  other arithmetic  12.1 us (9%)
  matrix products  6.06 us (4%)
  starting transfers between devices  5.1 us (4%)
  local copies, waits for them, and re-layouts  2.86 us (2%)
    psum x1, waiting for transfers between devices, shards(): lax.psum(partial_value, ('dp', 'sub')).astype(jnp.float32)  60.3 us
    pmax x1, blocking collectives, shards(): row_peak = lax.pmax(local_peak, 'cent')  9.84 us
    psum x1, blocking collectives, shards(): lax.psum(jnp.sum(jnp.exp(scores - row_peak[:, None]), axis=1), 'cent')  8.87 us
    unnamed x1, blocking collectives  8.72 us
    psum x1, blocking collectives, shards(): lax.psum(weight_mass, ('dp', 'sub')).astype(jnp.float32)  5.64 us
    reduce_sum x3, other arithmetic, normalize(): jnp.sum(floats * floats, axis=-1, keepdims=True) + 1e-06  5.22 us
    ppermute x1, starting transfers between devices, save_rates(): jax.lax.ppermute(carry_out[-1] if carry_out else m, comm_axis, perm=pool)  5.05 us
  transfers between devices with their start and end apart: 4, of which 2 were waited for; matrix products, arithmetic and copies ran while one was open for 5% of the time, Pallas kernels for 0%

profile of v1, /device:TPU:0, one launch (start us, length us, event | category | flops | bytes accessed | tf_op | source)
XLA Modules:
  0.0 136.5 jit_solution(15673804480127829627)
XLA Ops:
  7.2 0.0 all-reduce.3.cloned.1.call-start
  7.2 0.9 fusion.2
  8.1 0.9 fusion.3
  9.0 5.1 %collective-permute-start.2 = (bf16[32,768]{1,0:T(8,128)(2,1)S(1)}, bf16[32,768]{1,0:T(8,128)(2,1)S(1)}, u32[]{:S(2)}, u32[]{:S(2)}) collective-permute-start(bf16[32,768]{1,0:T(8,128)(2,1)S(1)} %fusion.3), channel_id=1, source_target_pairs={{4,0},{8,4},{12,8},{0,12},{5,1},{9,5},{13,9},{1,13},{6,2},{10,6},{... | collective-permute-start | bytes 147464 | tf_op jit(solution)/shard_map/ppermute | solution.py:33
  14.1 0.0 collective-permute-start
  14.1 0.9 fusion.15
  14.9 0.0 copy-start
  15.0 2.7 %fusion = f32[2048]{0:T(1024)S(1)} fusion(bf16[2048,768]{1,0:T(8,128)(2,1)} %param.6), kind=kLoop, calls=%fused_computation.3 | loop fusion | flops 4716544 | bytes 3153920 | tf_op jit(solution)/shard_map/reduce_sum | solution.py:15
  17.7 0.1 copy-done
  17.8 0.0 copy-start.4
  17.8 0.0 copy-start.3
  17.8 0.6 fusion.1
  18.4 1.6 %collective-permute-done = bf16[32,768]{1,0:T(8,128)(2,1)S(1)} collective-permute-done((bf16[32,768]{1,0:T(8,128)(2,1)S(1)}, bf16[32,768]{1,0:T(8,128)(2,1)S(1)}, u32[]{:S(2)}, u32[]{:S(2)}) %collective-permute-start) | collective-permute-done | bytes 49184 | tf_op jit(solution)/shard_map/ppermute | solution.py:27
  20.0 0.0 collective-permute-start.1
  20.6 0.0 copy-done.4
  20.6 0.6 dynamic-slice
  21.9 0.0 copy-done.3
  21.9 0.2 dynamic-update-slice
  22.1 8.7 %all-reduce = s32[128]{0:T(128)S(1)} all-reduce(s32[128]{0:T(128)S(1)} %dynamic-update-slice), channel_id=1, replica_groups=mesh['groups'=2,'cent'=4,'dp'=2,'sub'=2] {'cent'}, use_global_device_ids=true, to_apply=%add | all-reduce | flops 128 | bytes 1024
  30.9 0.0 collective-permute-done.2
  30.9 0.0 collective-permute-done.1
  30.9 0.6 gather_fusion
  31.5 2.1 %fusion.9 = (f32[128]{0:T(128)S(1)}, f32[128,2048]{1,0:T(8,128)}) fusion(f32[]{:T(128)} %bitcast.16, bf16[128,768]{1,0:T(8,128)(2,1)S(1)} %bitcast.18, bf16[2048,768]{1,0:T(8,128)(2,1)S(1)} %fusion.1), kind=kOutput, calls=%fused_computation.34 | convolution fusion | flops 403177344 | bytes 4391428 | tf_op jit(solution)/shard_map/dot_general | solution.py:49
  33.6 9.8 %pmax.7 = f32[128]{0:T(128)S(1)} all-reduce(f32[128]{0:T(128)S(1)} %get-tuple-element.7), channel_id=1, replica_groups=mesh['groups'=2,'cent'=4,'dp'=2,'sub'=2] {'cent'}, use_global_device_ids=true, to_apply=%region_3.4 | all-reduce | flops 128 | bytes 1024 | tf_op jit(solution)/shard_map/pmax | solution.py:55
  43.4 1.5 %exponential_reduce_fusion = f32[128]{0:T(128)S(1)} fusion(f32[128,2048]{1,0:T(8,128)} %get-tuple-element.8, f32[128]{0:T(128)S(1)} %pmax.7), kind=kLoop, calls=%fused_computation.11 | loop fusion | flops 524160 | bytes 1049600 | tf_op jit(solution)/shard_map/reduce_sum | solution.py:56
  45.0 8.9 %psum.21 = f32[128]{0:T(128)S(1)} all-reduce(f32[128]{0:T(128)S(1)} %exponential_reduce_fusion), channel_id=1, replica_groups=mesh['groups'=2,'cent'=4,'dp'=2,'sub'=2] {'cent'}, use_global_device_ids=true, to_apply=%region_5.6 | all-reduce | flops 128 | bytes 1024 | tf_op jit(solution)/shard_map/psum | solution.py:56
  53.8 1.5 %multiply_convert_fusion.1 = bf16[128,2048]{1,0:T(8,128)(2,1)S(1)} fusion(f32[128,2048]{1,0:T(8,128)} %get-tuple-element.8, f32[128]{0:T(128)S(1)} %get-tuple-element.4, f32[128]{0:T(128)S(1)} %convert_element_type.36), kind=kLoop, calls=%fused_computation.10 | loop fusion | flops 786432 | bytes 1573888 | tf_op jit(solution)/shard_map/convert_element_type | solution.py:59
  55.3 0.0 copy-start.2
  55.4 0.8 copy-done.2
  56.1 2.7 %convolution_convert_fusion = bf16[2048,768]{1,0:T(8,128)(2,1)} fusion(bf16[128,2048]{1,0:T(8,128)(2,1)S(1)} %multiply_convert_fusion.1, bf16[128,768]{1,0:T(8,128)(2,1)S(1)} %bitcast.19), kind=kOutput, calls=%fused_computation.5 | convolution fusion | flops 404226048 | bytes 3866624 | tf_op jit(solution)/shard_map/dot_general | solution.py:62
  58.9 0.0 all-reduce.3.cloned.1.call-update
  58.9 1.2 fusion.6
  60.1 0.6 dynamic_slice.15
  60.7 5.6 %psum.23 = bf16[2048]{0:T(1024)(128)(2,1)S(1)} all-reduce(bf16[2048]{0:T(1024)(128)(2,1)S(1)} %convert_element_type.45), channel_id=1, replica_groups=mesh['groups'=2,'cent'=4,'dp'=2,'sub'=2] {'dp','sub'}, use_global_device_ids=true, to_apply=%region_7.8 | all-reduce | flops 2048 | bytes 8192 | tf_op jit(solution)/shard_map/psum | solution.py:73
  66.3 0.1 convert_add_fusion
  66.4 60.3 %all-reduce.3.cloned.1.call-done = bf16[2048,768]{1,0:T(8,128)(2,1)} async-done(((bf16[2048,768]{1,0:T(8,128)(2,1)}), bf16[2048,768]{1,0:T(8,128)(2,1)}) %all-reduce.3.cloned.1.call-update) | async-done | bytes 3145744 | tf_op jit(solution)/shard_map/psum | solution.py:72
  126.7 1.6 %multiply_reduce_fusion = (f32[512]{0:T(512)S(1)}, f32[512,768]{1,0:T(8,128)S(1)}) fusion(f32[512]{0:T(512)S(1)} %convert_add_fusion, bf16[2048,768]{1,0:T(8,128)(2,1)S(1)} %fusion.1, s32[]{:T(128)S(6)} %select_n.34, bf16[2048,768]{1,0:T(8,128)(2,1)} %all-reduce.3.cloned.1.call-done), kind=kLoop, calls=%fused_computation.8 | loop fusion | flops 2358784 | bytes 3149828 | tf_op jit(solution)/shard_map/reduce_sum | solution.py:15
  128.3 0.0 copy-start.1
  128.3 1.4 %multiply_convert_fusion = bf16[512,768]{1,0:T(8,128)(2,1)} fusion(f32[512]{0:T(512)S(1)} %add_rsqrt_fusion.1, f32[512,768]{1,0:T(8,128)S(1)} %get-tuple-element.6, f32[512]{0:T(512)S(1)} %convert_add_fusion, bf16[2048,768]{1,0:T(8,128)(2,1)S(1)} %fusion.1, s32[]{:T(128)S(6)} %select_n.34), kind=kLoop, calls=%fused_computation.7 | loop fusion | flops 1966080 | bytes 3149828 | tf_op jit(solution)/shard_map/convert_element_type | solution.py:79
  129.7 0.0 copy-done.1
  (10 shorter events, 0.1 us)
Async XLA Ops:
  7.2 119.5 %all-reduce.3.cloned.1.call-start = ((), (), s32[]{:S(2)}) async-start(), calls=%async_computation | async-start | bytes 6291456 | tf_op jit(solution)/shard_map/psum | solution.py:72
  9.0 21.8 %collective-permute-start.2 = (bf16[32,768]{1,0:T(8,128)(2,1)S(1)}, bf16[32,768]{1,0:T(8,128)(2,1)S(1)}, u32[]{:S(2)}, u32[]{:S(2)}) collective-permute-start(bf16[32,768]{1,0:T(8,128)(2,1)S(1)} %fusion.3), channel_id=1, source_target_pairs={{4,0},{8,4},{12,8},{0,12},{5,1},{9,5},{13,9},{1,13},{6,2},{10,6},{... | collective-permute-start | bytes 147464 | tf_op jit(solution)/shard_map/ppermute | solution.py:33
  14.1 5.9 %collective-permute-start = (bf16[32,768]{1,0:T(8,128)(2,1)S(1)}, bf16[32,768]{1,0:T(8,128)(2,1)S(1)}, u32[]{:S(2)}, u32[]{:S(2)}) collective-permute-start(bf16[32,768]{1,0:T(8,128)(2,1)S(1)} %fusion.3), channel_id=1, source_target_pairs={{0,4},{4,8},{8,12},{12,0},{1,5},{5,9},{9,13},{13,1},{2,6},{6,10},{... | collective-permute-start | bytes 147464 | tf_op jit(solution)/shard_map/ppermute | solution.py:27
  14.9 2.8 %copy-start = (bf16[2048,768]{1,0:T(8,128)(2,1)S(1)}, bf16[2048,768]{1,0:T(8,128)(2,1)}, u32[]{:S(2)}) copy-start(bf16[2048,768]{1,0:T(8,128)(2,1)} %param.6) | copy-start | bytes 9437188
  17.8 2.8 %copy-start.4 = (u32[32]{0:T(128)S(1)}, u32[32]{0:T(128)}, u32[]{:S(2)}) copy-start(u32[32]{0:T(128)} %constant.55) | copy-start | bytes 388
  17.8 4.1 %copy-start.3 = (s32[32]{0:T(128)S(1)}, s32[32]{0:T(128)}, u32[]{:S(2)}) copy-start(s32[32]{0:T(128)} %param.5) | copy-start | bytes 388
  20.0 10.9 %collective-permute-start.1 = (bf16[32,768]{1,0:T(8,128)(2,1)S(1)}, bf16[32,768]{1,0:T(8,128)(2,1)S(1)}, u32[]{:S(2)}, u32[]{:S(2)}) collective-permute-start(bf16[32,768]{1,0:T(8,128)(2,1)S(1)} %collective-permute-done), channel_id=1, source_target_pairs={{0,4},{4,8},{8,12},{12,0},{1,5},{5,9},{9,13},{13,1},{2,6},{6,10},{... | collective-permute-start | bytes 147464 | tf_op jit(solution)/shard_map/ppermute | solution.py:27
  55.3 0.8 copy-start.2
  128.3 1.4 %copy-start.1 = (f32[512,768]{1,0:T(8,128)}, f32[512,768]{1,0:T(8,128)S(1)}, u32[]{:S(2)}) copy-start(f32[512,768]{1,0:T(8,128)S(1)} %get-tuple-element.6) | copy-start | bytes 4718596
Sparse Core Ops, SparseCore 0:
  59.0 67.6 all-reduce.2
